TPU v7x, 512 devices: a whole 4x4x16 slice. The times are simulated.
512 devices in a mesh: col: 32 (over y, x, core), row: 16 (over z).
Axes of the slice: x: 4, y: 4, z: 16, core: 2. Of those that a mesh axis runs over, the one named last changes fastest.
Arguments:
- normal_matrix: float32 [4, 16, 128, 2, 32, 128], P(None, 'row', None, None, 'col'), may hold values from -3 to 5.5, as said below
- right_sides: float32 [256, 4, 16, 128], P('col', None, 'row'), may hold values from -6 to 6
Outputs:
- reduced_matrix: float32 [4, 16, 128, 2, 32, 128], P(None, 'row', None, None, 'col')
- reduced_sides: float32 [256, 4, 16, 128], P('col', None, 'row')
Inputs may be any that keep to these rules, and one draw needn't show every extreme that they name: `normal_matrix`: A is symmetric; its leading 128 x 128 block is strictly diagonally dominant with a positive diagonal.
All inputs are finite; a program needn't handle non-finite values.
Results may differ from a plain program's by a relative error of at most 0.00005.
Values sent between devices are 32-bit elements; how exact they have to be, the bound alone decides.
No kernel may reach another device: no remote copies, remote signals or barrier semaphores. Data moves between devices by JAX's collectives and lax.ppermute only.
A program may use at most 64 MiB of HBM per device.

v0:
```python
import jax
import jax.numpy as jnp
from jax import lax
from jax.sharding import PartitionSpec as P


def spread(block, axis, holder):
    block = jnp.where(lax.axis_index(axis) == holder, block, jnp.zeros_like(block))
    return lax.psum(block, axis)


def on_device(normal_matrix, right_sides):
    row_blocks, _, block, col_blocks, _, _ = normal_matrix.shape
    col_id = lax.axis_index("col")
    row_id = lax.axis_index("row")
    col_count = lax.axis_size("col")
    row_count = lax.axis_size("row")
    local = normal_matrix.reshape(row_blocks * block, col_blocks * block)
    first = local[:, :block]
    corner_raw = spread(first[:block], "row", 0)
    identity = jnp.eye(block, dtype=jnp.float32)
    corner_raw = jnp.where(col_id == 0, corner_raw, identity)
    corner_own = jnp.linalg.cholesky(corner_raw)
    rows_own = jax.scipy.linalg.solve_triangular(corner_own, first.T, lower=True).T
    stacked = jnp.concatenate([corner_own, rows_own], axis=0)
    stacked = spread(stacked, "col", 0)
    corner = stacked[:block]
    rows_factor = stacked[block:]
    picked = []
    for index in range(col_blocks):
        start = (index * col_count + col_id) // row_count * block
        picked.append(lax.dynamic_slice_in_dim(rows_factor, start, block, 0))
    selected = jnp.concatenate(picked, axis=0)
    cols_factor = spread(selected, "row", col_id % row_count)
    change = jnp.dot(
        rows_factor,
        cols_factor.T,
        precision=lax.Precision.HIGHEST,
        preferred_element_type=jnp.float32,
    )
    trailing = (local - change).reshape(row_blocks, block, col_blocks, block)
    global_rows = row_id + row_count * jnp.arange(row_blocks, dtype=jnp.int32)
    global_cols = col_id + col_count * jnp.arange(col_blocks, dtype=jnp.int32)
    inner = (global_rows[:, None, None, None] >= 1) & (global_cols[None, None, :, None] >= 1)
    result = jnp.where(inner, trailing, jnp.float32(0.0))
    column = jnp.where(
        global_rows[:, None, None] == 0, corner[None], rows_factor.reshape(row_blocks, block, block)
    )
    result = jnp.where((global_cols == 0)[None, None, :, None], column[:, :, None, :], result)
    result = result.reshape(normal_matrix.shape)
    side_count = right_sides.shape[0]
    top_sides = spread(right_sides[:, 0, 0, :], "row", 0)
    lead = jax.scipy.linalg.solve_triangular(corner, top_sides.T, lower=True).T
    flat = right_sides.reshape(side_count, row_blocks * block)
    reduced = flat - jnp.dot(
        lead, rows_factor.T, precision=lax.Precision.HIGHEST, preferred_element_type=jnp.float32
    )
    reduced = reduced.reshape(side_count, row_blocks, block)
    reduced = jnp.where((global_rows == 0)[None, :, None], lead[:, None, :], reduced)
    return (result, reduced.reshape(right_sides.shape))


def solution(mesh):
    placed = (P(None, "row", None, None, "col", None), P("col", None, "row", None))
    return jax.shard_map(
        on_device,
        mesh=mesh,
        in_specs=placed,
        out_specs=(P(None, "row", None, None, "col", None), P("col", None, "row", None)),
        check_vma=False,
    )
```

profile of v0, /device:TPU:2, one launch (start us, length us, event | category | flops | bytes accessed | tf_op | source)
XLA Modules:
  0.0 458.6 jit_solution(13755997180216444617)
XLA Ops:
  7.2 0.0 all-reduce.4.cloned.1.call-start
  7.2 1.1 copy.16
  8.3 0.6 slice_select_fusion
  8.9 0.0 copy-start.3
  8.9 0.0 all-reduce.4.cloned.1.call-update
  9.0 0.0 all-reduce.6.cloned.1.call-start
  9.0 0.6 copy-done.3
  9.7 0.1 broadcast_and_fusion
  9.7 139.2 %all-reduce.4.cloned.1.call-done = f32[128,128]{1,0:T(8,128)} async-done(((f32[128,128]{1,0:T(8,128)}), f32[128,128]{1,0:T(8,128)}) %all-reduce.4.cloned.1.call-update) | async-done | bytes 65552 | tf_op jit(solution)/shard_map/psum | solution.py:9
  149.0 0.0 copy-start.2
  149.0 0.1 copy.4
  149.1 0.7 copy-done.2
  149.9 11.7 %cholesky.19 = f32[128,128]{1,0:T(8,128)S(1)} custom-call(f32[128,128]{1,0:T(8,128)S(1)} %fusion.5), custom_call_target="Cholesky" | custom-call | tf_op jit(solution)/shard_map/jit(cholesky)/cholesky | solution.py:23
  161.6 0.6 compare_reduce_fusion
  162.2 0.7 select_bitcast_fusion.1
  162.9 9.8 %custom-call.11 = f32[1,128,128]{1,2,0:T(8,128)S(1)} custom-call(f32[1,128,128]{2,1,0:T(8,128)S(1)} %get-tuple-element.2), custom_call_target="InvertDiagBlocksLowerTriangular" | custom-call | tf_op jit(solution)/shard_map/jit(_solve_triangular)/triangular_solve | solution.py:24
  172.7 0.4 convolution_bitcast_fusion
  173.1 0.7 maximum_select_fusion
  173.8 0.0 all-reduce.6.cloned.1.call-update
  173.9 0.0 all-reduce.8.cloned.1.call-start
  174.0 27.5 %psum.31 = f32[8,128]{1,0:T(8,128)S(1)} all-reduce(f32[8,128]{1,0:T(8,128)S(1)} %bitcast.46), channel_id=1, replica_groups=mesh['col'=32,'row'=16] {'row'}, use_global_device_ids=true, to_apply=%region_5.6 | all-reduce | flops 1024 | bytes 8192 | tf_op jit(solution)/shard_map/psum | solution.py:9
  201.5 100.2 %all-reduce.6.cloned.1.call-done = f32[640,128]{1,0:T(8,128)} async-done(((f32[640,128]{1,0:T(8,128)}), f32[640,128]{1,0:T(8,128)}) %all-reduce.6.cloned.1.call-update) | async-done | bytes 327696 | tf_op jit(solution)/shard_map/psum | solution.py:9
  301.7 0.8 select_bitcast_fusion
  302.5 9.8 %custom-call.12 = f32[1,128,128]{1,2,0:T(8,128)S(1)} custom-call(f32[1,128,128]{2,1,0:T(8,128)S(1)} %get-tuple-element.4), custom_call_target="InvertDiagBlocksLowerTriangular" | custom-call | tf_op jit(solution)/shard_map/jit(_solve_triangular)/triangular_solve | solution.py:53
  312.4 1.0 slice.42
  313.4 0.7 maximum_select_fusion.1
  314.0 0.0 all-reduce.8.cloned.1.call-update
  314.0 0.0 copy-start
  314.1 0.0 copy-start.1
  314.1 0.2 fusion.2
  314.2 0.1 broadcast_select_fusion.2
  314.3 0.7 copy-done
  315.0 0.3 fusion
  315.3 0.7 broadcast_select_fusion.3
  316.0 132.8 %all-reduce.8.cloned.1.call-done = f32[256,128]{1,0:T(8,128)} async-done(((f32[256,128]{1,0:T(8,128)}), f32[256,128]{1,0:T(8,128)}) %all-reduce.8.cloned.1.call-update) | async-done | bytes 131088 | tf_op jit(solution)/shard_map/psum | solution.py:9
  448.8 0.0 copy-done.1
  448.8 1.5 convolution_subtract_fusion
  450.3 0.3 reshape.136
  450.6 1.5 broadcast_select_fusion
  (9 shorter events, 0.1 us)
Async XLA Ops:
  7.2 141.8 %all-reduce.4.cloned.1.call-start = ((), (), s32[]{:S(2)}) async-start(), calls=%async_computation | async-start | bytes 131072 | tf_op jit(solution)/shard_map/psum | solution.py:9
  8.9 0.7 copy-start.3
  9.0 292.7 %all-reduce.6.cloned.1.call-start = ((), (), s32[]{:S(2)}) async-start(), calls=%async_computation.1 | async-start | bytes 655360 | tf_op jit(solution)/shard_map/psum | solution.py:9
  149.0 0.8 copy-start.2
  173.9 274.9 %all-reduce.8.cloned.1.call-start = ((), (), s32[]{:S(2)}) async-start(), calls=%async_computation.2 | async-start | bytes 262144 | tf_op jit(solution)/shard_map/psum | solution.py:9
  314.0 1.0 copy-start
  314.1 134.7 %copy-start.1 = (f32[4,1,128,2,1,128]{5,4,3,2,1,0:T(1,128)S(1)}, f32[4,1,128,2,1,128]{5,4,3,2,1,0:T(1,128)}, u32[]{:S(2)}) copy-start(f32[4,1,128,2,1,128]{5,4,3,2,1,0:T(1,128)} %param.2) | copy-start | bytes 1572868
Sparse Core Ops, SparseCore 0:
  10.9 138.0 all-reduce.3
  174.0 127.6 all-reduce.5
  314.2 134.5 all-reduce.7
where the time goes:
time: 459 us
  waiting for transfers between devices  372 us (81%)
  other arithmetic  38 us (8%)
  blocking collectives  27.5 us (6%)
  between operations  13.9 us (3%)
    psum x3, waiting for transfers between devices, spread(): return lax.psum(block, axis)  372 us
    psum x1, blocking collectives, spread(): return lax.psum(block, axis)  27.5 us
    another operation x3, other arithmetic, on_device(): corner_own = jnp.linalg.cholesky(corner_raw)  12.4 us
    another operation x2, other arithmetic, on_device(): lead = jax.scipy.linalg.solve_triangular(corner, top_sides.T, lower=True).T  10.7 us
    another operation x2, other arithmetic, on_device(): jax.scipy.linalg.solve_triangular(corner_own, first.T, lower=True)  10.5 us
  transfers between devices with their start and end apart: 3, of which 3 were waited for; matrix products, arithmetic and copies ran while one was open for 0% of the time, Pallas kernels for 0%

commit v1 on v0

--- a/solution.py
+++ b/solution.py
@@ -6,7 +6,7 @@
 
 def spread(block, axis, holder):
     block = jnp.where(lax.axis_index(axis) == holder, block, jnp.zeros_like(block))
-    return lax.psum(block, axis)
+    return jnp.sum(lax.all_gather(block, axis), axis=0)
 
 
 def on_device(normal_matrix, right_sides):

time: 459 us -> 272 us (0.59)
  waiting for transfers between devices: 372 us -> 179 us
  other arithmetic: 38 us -> 44 us
    psum x3 -> x0, waiting for transfers between devices: 372 us -> none  [spread(): return lax.psum(block, axis)]
    all_gather x0 -> x3, waiting for transfers between devices: none -> 178 us  [spread(): return jnp.sum(lax.all_gather(block, axis), axis=0)]
    all_gather x0 -> x1, blocking collectives: none -> 30.7 us  [spread(): return jnp.sum(lax.all_gather(block, axis), axis=0)]
    psum x1 -> x0, blocking collectives: 27.5 us -> none  [spread(): return lax.psum(block, axis)]
    reduce_sum x0 -> x4, other arithmetic: none -> 7.48 us  [spread(): return jnp.sum(lax.all_gather(block, axis), axis=0)]
    another operation x2 -> x1, other arithmetic: 10.5 us -> 9.81 us  [on_device(): jax.scipy.linalg.solve_triangular(corner_own, first.T, lower=True)]
  transfers between devices with their start and end apart: 3 -> 3, of which waited for: 3 -> 3; matrix products, arithmetic and copies ran while one was open for 0% -> 4% of each run, Pallas kernels for 0% -> 0%
where the time goes in v1:
time: 272 us
  waiting for transfers between devices  179 us (66%)
  other arithmetic  44 us (16%)
  blocking collectives  30.7 us (11%)
  between operations  14 us (5%)
  local copies, waits for them, and re-layouts  3.09 us (1%)
    all_gather x3, waiting for transfers between devices, spread(): return jnp.sum(lax.all_gather(block, axis), axis=0)  178 us
    all_gather x1, blocking collectives, spread(): return jnp.sum(lax.all_gather(block, axis), axis=0)  30.7 us
    another operation x3, other arithmetic, on_device(): corner_own = jnp.linalg.cholesky(corner_raw)  12.4 us
    another operation x2, other arithmetic, on_device(): lead = jax.scipy.linalg.solve_triangular(corner, top_sides.T, lower=True).T  9.82 us
    another operation x1, other arithmetic, on_device(): jax.scipy.linalg.solve_triangular(corner_own, first.T, lower=True)  9.81 us
    reduce_sum x4, other arithmetic, spread(): return jnp.sum(lax.all_gather(block, axis), axis=0)  7.48 us
  transfers between devices with their start and end apart: 3, of which 3 were waited for; matrix products, arithmetic and copies ran while one was open for 4% of the time, Pallas kernels for 0%

profile of v1, /device:TPU:2, one launch (start us, length us, event | category | flops | bytes accessed | tf_op | source)
XLA Modules:
  0.0 271.9 jit_solution(14735918429483486960)
XLA Ops:
  7.2 0.0 copy-start.1
  7.2 0.0 all-gather.10.cloned.1.call-start
  7.2 1.1 copy.39
  8.3 0.6 slice_select_fusion
  8.9 0.0 all-gather.10.cloned.1.call-update
  9.0 0.0 all-gather.6.cloned.1.call-start
  9.0 77.1 %all-gather.10.cloned.1.call-done = f32[2048,128]{1,0:T(8,128)} async-done(((f32[128,128]{1,0:T(8,128)}), f32[2048,128]{1,0:T(8,128)}) %all-gather.10.cloned.1.call-update) | async-done | bytes 1048592 | tf_op jit(solution)/shard_map/all_gather | solution.py:9
  86.2 1.3 reduce_sum.38
  87.5 0.0 copy-start
  87.5 0.1 copy.17
  87.6 11.7 %cholesky.19 = f32[128,128]{1,0:T(8,128)S(1)} custom-call(f32[128,128]{1,0:T(8,128)S(1)} %fusion.6), custom_call_target="Cholesky" | custom-call | tf_op jit(solution)/shard_map/jit(cholesky)/cholesky | solution.py:23
  99.3 0.6 compare_reduce_fusion
  100.0 0.7 fusion.7
  100.7 9.8 %custom-call.11 = f32[1,128,128]{1,2,0:T(8,128)S(1)} custom-call(f32[1,128,128]{2,1,0:T(8,128)S(1)} %get-tuple-element.7), custom_call_target="InvertDiagBlocksLowerTriangular" | custom-call | tf_op jit(solution)/shard_map/jit(_solve_triangular)/triangular_solve | solution.py:24
  110.5 0.4 convolution_bitcast_fusion
  110.9 0.1 copy.18
  111.0 0.9 copy.19
  111.9 0.0 all-gather.6.cloned.1.call-update
  111.9 0.0 all-gather.8.cloned.1.call-start
  112.0 70.1 %all-gather.6.cloned.1.call-done = f32[32,640,128]{2,1,0:T(8,128)} async-done(((f32[1,640,128]{2,1,0:T(8,128)}), f32[32,640,128]{2,1,0:T(8,128)}) %all-gather.6.cloned.1.call-update) | async-done | bytes 10485776 | tf_op jit(solution)/shard_map/all_gather | solution.py:9
  182.1 4.5 %reduce_sum.40 = f32[640,128]{1,0:T(8,128)S(1)} reduce(f32[32,640,128]{2,1,0:T(8,128)} %all-gather.6.cloned.1.call-done, f32[]{:T(128)} %constant.100.clone.1), dimensions={0}, to_apply=%region_3.4 | reduce | flops 2539520 | bytes 10813444 | tf_op jit(solution)/shard_map/reduce_sum | solution.py:9
  186.6 0.1 copy.31
  186.8 0.1 copy.24
  186.9 0.1 copy.25
  187.0 0.7 maximum_select_fusion.1
  187.7 0.0 all-gather.8.cloned.1.call-update
  187.7 0.0 copy-done.1
  187.7 30.7 %all-gather.1 = f32[128,1,1,128]{3,2,1,0:T(1,128)S(1)} all-gather(f32[8,1,1,128]{3,2,1,0:T(1,128)S(1)} %broadcast_select_fusion.4), channel_id=3, replica_groups=mesh['col'=32,'row'=16] {'row'}, dimensions={0}, use_global_device_ids=true | all-gather | bytes 69632 | tf_op jit(solution)/shard_map/all_gather | solution.py:9
  218.5 0.1 broadcast_and_fusion
  218.6 0.1 reshape.203
  218.7 9.8 %custom-call.12 = f32[1,128,128]{1,2,0:T(8,128)S(1)} custom-call(f32[1,128,128]{2,1,0:T(8,128)S(1)} %get-tuple-element.2), custom_call_target="InvertDiagBlocksLowerTriangular" | custom-call | tf_op jit(solution)/shard_map/jit(_solve_triangular)/triangular_solve | solution.py:53
  228.5 0.1 copy.30
  228.6 0.1 broadcast_select_fusion.2
  228.7 0.1 copy.23
  228.9 0.2 fusion.2
  229.0 0.3 fusion
  229.4 0.7 broadcast_select_fusion.3
  230.1 31.2 %all-gather.8.cloned.1.call-done = f32[16,256,128]{2,1,0:T(8,128)} async-done(((f32[1,256,128]{2,1,0:T(8,128)}), f32[16,256,128]{2,1,0:T(8,128)}) %all-gather.8.cloned.1.call-update) | async-done | bytes 2097168 | tf_op jit(solution)/shard_map/all_gather | solution.py:9
  261.3 1.7 reduce_sum.41
  263.0 0.0 copy-done
  263.0 0.6 convolution_subtract_fusion
  263.6 0.3 reshape.204
  263.9 1.5 broadcast_select_fusion
  (12 shorter events, 0.2 us)
Async XLA Ops:
  7.2 180.6 %copy-start.1 = (f32[8,4,1,128]{3,2,1,0:T(1,128)S(1)}, f32[8,4,1,128]{3,2,1,0:T(1,128)}, u32[]{:S(2)}) copy-start(f32[8,4,1,128]{3,2,1,0:T(1,128)} %param.3) | copy-start | bytes 49156
  7.2 79.0 %all-gather.10.cloned.1.call-start = ((), (), s32[]{:S(2)}) async-start(), calls=%async_computation.2 | async-start | bytes 1114112 | tf_op jit(solution)/shard_map/all_gather | solution.py:9
  9.0 173.2 %all-gather.6.cloned.1.call-start = ((), (), s32[]{:S(2)}) async-start(), calls=%async_computation | async-start | bytes 10813440 | tf_op jit(solution)/shard_map/all_gather | solution.py:9
  87.5 175.5 %copy-start = (f32[4,1,128,2,1,128]{5,4,3,2,1,0:T(1,128)S(1)}, f32[4,1,128,2,1,128]{5,4,3,2,1,0:T(1,128)}, u32[]{:S(2)}) copy-start(f32[4,1,128,2,1,128]{5,4,3,2,1,0:T(1,128)} %param.2) | copy-start | bytes 1572868
  111.9 149.3 %all-gather.8.cloned.1.call-start = ((), (), s32[]{:S(2)}) async-start(), calls=%async_computation.1 | async-start | bytes 2228224 | tf_op jit(solution)/shard_map/all_gather | solution.py:9
Sparse Core Ops, SparseCore 0:
  10.7 75.4 all-gather.9
  112.1 70.0 all-gather.5
  187.8 73.3 all-gather.7
